TPU v7x, 512 devices: a whole 4x8x8 slice. The times are simulated.
512 devices in a mesh: req: 128 (over z, y, core), grp: 4 (over x).
Axes of the slice: x: 4, y: 8, z: 8, core: 2. Of those that a mesh axis runs over, the one named last changes fastest.
Arguments:
- owner_slab: bfloat16 [65536, 1024], P('req'), may hold values from -6 to 6
- segment_ids: int32 [128, 512], P('req'), may hold values from 0 to 511, as said below
- head_weights: bfloat16 [1024, 16, 192], P(None, 'grp')
- merge_weights: bfloat16 [16, 64, 1024], P('grp'), may hold values from -0.1875 to 0.1875
- first_gain: float32 [1024], replicated, may hold values from 0.25 to 1.75
- first_bias: float32 [1024], replicated, may hold values from -3 to 3
- up_weights: bfloat16 [1024, 4096], P('req', 'grp'), may hold values from -0.1875 to 0.1875
- down_weights: bfloat16 [4096, 1024], P('grp', 'req'), may hold values from -0.09375 to 0.09375
- second_gain: float32 [1024], replicated, may hold values from 0.25 to 1.75
- second_bias: float32 [1024], replicated, may hold values from -3 to 3
- page_table: int32 [128, 4], P('req'), may hold values from 0 to 3, each once within a row
- row_map: int32 [128, 4, 128], P('req', 'grp'), may hold values from 0 to 127, each once within a row
Outputs:
- layer_out: bfloat16 [65536, 1024], P(('req', 'grp'))
- cache_pages: bfloat16 [512, 128, 16, 128], P('req', None, 'grp')
Inputs may be any that keep to these rules, and one draw needn't show every extreme that they name: `segment_ids`: within each slab the ids start at 0, never fall and rise by at most one from row to row; in one slab all 512 rows form a single request, and in one other slab every row is a request of its own.
All inputs are finite; a program needn't handle non-finite values.
Results may differ from a plain program's by a relative error of at most 0.0075.
Values may be sent and summed in bfloat16 or wider, within the bound.
No kernel may reach another device: no remote copies, remote signals or barrier semaphores. Data moves between devices by JAX's collectives and lax.ppermute only.
A program may use at most 64 MiB of HBM per device.

v0:
```python
import math

import jax
import jax.numpy as jnp
from jax import lax
from jax.sharding import PartitionSpec as P

EPSILON = 1e-05


def layer_norm(values, gain, bias):
    center = values - jnp.mean(values, axis=-1, keepdims=True)
    spread = jnp.mean(center * center, axis=-1, keepdims=True)
    return center * lax.rsqrt(spread + EPSILON) * gain + bias


def local(
    owner_slab,
    segment_ids,
    head_weights,
    merge_weights,
    first_gain,
    first_bias,
    up_weights,
    down_weights,
    second_gain,
    second_bias,
    page_table,
    row_map,
):
    group = lax.axis_size("grp")
    owners = lax.axis_size("req")
    rows_all = owner_slab.shape[0]
    width = owner_slab.shape[1]
    quarter = rows_all // group
    local_heads = head_weights.shape[1]
    head_dim = head_weights.shape[2] // 3
    projected = jnp.einsum(
        "nd,dhc->nhc", owner_slab, head_weights, preferred_element_type=jnp.float32
    ).astype(jnp.bfloat16)
    queries = jnp.moveaxis(projected[:, :, :head_dim], 1, 0)
    key_rows = jnp.moveaxis(projected[:, :, head_dim : 2 * head_dim], 1, 0)
    value_rows = jnp.moveaxis(projected[:, :, 2 * head_dim :], 1, 0)
    segment = segment_ids[0]
    position = jnp.arange(rows_all, dtype=jnp.int32)
    allowed = (position[:, None] >= position[None, :]) & (segment[:, None] == segment[None, :])
    scale = 1.0 / math.sqrt(head_dim)

    def one_head(operands):
        query_head, key_head, value_head = operands
        scores = (
            lax.dot_general(
                query_head, key_head, (((1,), (1,)), ((), ())), preferred_element_type=jnp.float32
            )
            * scale
        )
        scores = jnp.where(allowed, scores, -1e30)
        probs = jax.nn.softmax(scores, axis=-1).astype(jnp.bfloat16)
        return jnp.dot(probs, value_head, preferred_element_type=jnp.float32).astype(jnp.bfloat16)

    attended = jnp.moveaxis(lax.map(one_head, (queries, key_rows, value_rows)), 0, 1)
    own = lax.axis_index("grp")
    own_rows = lax.dynamic_slice_in_dim(owner_slab, own * quarter, quarter, 0).astype(jnp.float32)
    partial_rows = jnp.einsum(
        "nhd,hde->ne", attended, merge_weights, preferred_element_type=jnp.float32
    )
    mixed = lax.psum_scatter(partial_rows, "grp", scatter_dimension=0, tiled=True)
    hidden = layer_norm(own_rows + mixed, first_gain, first_bias).astype(jnp.bfloat16)
    slots = quarter // owners
    placed = jnp.zeros_like(hidden).at[row_map[0, 0]].set(hidden)
    arrived = lax.all_to_all(
        placed.reshape(owners, slots, width), "req", split_axis=0, concat_axis=0, tiled=True
    )
    even_rows = arrived.reshape(quarter, width)
    group_rows = lax.all_gather(even_rows, "grp", axis=0, tiled=True)
    raised = jnp.dot(
        group_rows,
        lax.all_gather(up_weights, "req", axis=0, tiled=True),
        preferred_element_type=jnp.float32,
    )
    activated = jax.nn.gelu(raised, approximate=False).astype(jnp.bfloat16)
    lowered_all = jnp.dot(
        activated,
        lax.all_gather(down_weights, "req", axis=1, tiled=True),
        preferred_element_type=jnp.float32,
    )
    lowered = lax.psum_scatter(lowered_all, "grp", scatter_dimension=0, tiled=True)
    layer_out = layer_norm(
        even_rows.astype(jnp.float32) + lowered, second_gain, second_bias
    ).astype(jnp.bfloat16)
    page_count = page_table.shape[1]
    page_rows = rows_all // page_count
    stacked = projected[:, :, head_dim:].reshape(page_count, page_rows, local_heads, 2 * head_dim)
    cache_pages = jnp.zeros_like(stacked).at[page_table[0]].set(stacked)
    return (layer_out, cache_pages)


def solution(mesh):
    in_specs = (
        P("req", None),
        P("req", None),
        P(None, "grp", None),
        P("grp", None, None),
        P(),
        P(),
        P("req", "grp"),
        P("grp", "req"),
        P(),
        P(),
        P("req", None),
        P("req", "grp", None),
    )
    out_specs = (P(("req", "grp"), None), P("req", None, "grp", None))
    return jax.shard_map(local, mesh=mesh, in_specs=in_specs, out_specs=out_specs, check_vma=False)
```

profile of v0, /device:TPU:1, one launch (start us, length us, event | category | flops | bytes accessed | tf_op | source)
XLA Modules:
  0.0 281.3 jit_solution(15280526608803334837)
XLA Ops:
  8.0 0.0 copy-start
  8.0 0.0 reduce-scatter.3.cloned.1.call-start
  8.1 1.3 copy-done
  9.4 2.2 fusion.105
  11.6 0.0 copy-start.7
  11.7 0.1 convert_element_type.25
  11.8 0.1 slice_bitcast_fusion
  11.9 0.5 copy-done.7
  12.3 3.7 %while.11 = (s32[]{:T(128)}, bf16[4,512,64]{1,2,0:T(8,128)(2,1)S(1)}, bf16[4,512,64]{1,2,0:T(8,128)(2,1)S(1)}, bf16[4,512,64]{1,2,0:T(8,128)(2,1)S(1)}, bf16[4,5...) while((s32[]{:T(128)}, bf16[4,512,64]{1,2,0:T(8,128)(2,1)S(1)}, ...), condition=%wide.region_3.4_spmd.clone, body=%wide.region_0.3_spmd.clone.sunk | while | flops 70024192 | bytes 3424341 | solution.py:61
  12.3 0.4 fusion.116
  12.7 0.2 fusion.117
  12.9 0.3 fusion.118
  13.3 0.4 fusion.116
  13.7 0.2 fusion.117
  13.9 0.3 fusion.118
  14.2 0.4 fusion.116
  14.6 0.2 fusion.117
  14.8 0.3 fusion.118
  15.1 0.4 fusion.116
  15.6 0.2 fusion.117
  15.8 0.3 fusion.118
  16.1 0.0 copy-start.10
  16.1 0.7 copy-done.10
  16.8 3.0 %convolution_bitcast_fusion = f32[512,1024]{1,0:T(8,128)} fusion(bf16[4,64,1024]{2,1,0:T(8,128)(2,1)} %param.17, bf16[4,512,64]{1,2,0:T(8,128)(2,1)} %copy-done.10), kind=kOutput, calls=%fused_computation.40 | convolution fusion | flops 268435456 | bytes 2883584 | tf_op jit(solution)/shard_map/nhd,hde->ne/dot_general | solution.py:64
  19.8 0.0 reduce-scatter.3.cloned.1.call-update
  19.8 0.0 all-gather.5.cloned.1.call-start
  19.9 0.5 all-gather.5.cloned.1.call-update
  20.4 0.0 all-gather.7.cloned.1.call-start
  20.4 0.5 all-gather.7.cloned.1.call-update
  21.0 0.0 all-gather.9.cloned.1.call-start
  21.0 0.0 copy-done.8
  21.1 39.4 %reduce-scatter.3.cloned.1.call-done = f32[128,1024]{1,0:T(8,128)} async-done(((f32[512,1024]{1,0:T(8,128)}), f32[128,1024]{1,0:T(8,128)}) %reduce-scatter.3.cloned.1.call-update) | async-done | bytes 524304 | tf_op jit(solution)/shard_map/reduce_scatter | solution.py:67
  60.4 0.0 copy-done.2
  60.4 1.2 fusion.70
  61.6 1.2 multiply_reduce_fusion.1
  62.9 0.0 copy-done.3
  62.9 0.0 copy-done.4
  62.9 1.9 scatter_custom_fusion
  64.8 0.5 broadcast.106
  65.3 0.8 reduce
  66.1 0.2 reshape.126
  66.3 30.1 %all_to_all.5 = bf16[128,2,512]{2,1,0:T(2,128)(2,1)S(1)} all-to-all(bf16[128,2,512]{2,1,0:T(2,128)(2,1)S(1)} %reshape.126), channel_id=1, replica_groups=mesh['req'=128,'grp'=4] {'req'}, dimensions={0} | all-to-all | bytes 524288 | tf_op jit(solution)/shard_map/all_to_all | solution.py:71
  96.4 0.2 reshape.127
  96.6 0.8 copy.29
  97.4 0.0 all-gather.9.cloned.1.call-update
  97.4 0.2 reduce-scatter.5.cloned.1.call-start
  97.7 16.5 %all-gather.5.cloned.1.call-done = bf16[1024,1024]{1,0:T(8,128)(2,1)} async-done(((bf16[8,1024]{1,0:T(8,128)(2,1)}), bf16[1024,1024]{1,0:T(8,128)(2,1)}) %all-gather.5.cloned.1.call-update) | async-done | bytes 2097168 | tf_op jit(solution)/shard_map/all_gather | solution.py:78
  114.2 82.0 %all-gather.7.cloned.1.call-done = bf16[1024,1024]{0,1:T(8,128)(2,1)} async-done(((bf16[1024,8]{0,1:T(8,128)(2,1)}), bf16[1024,1024]{0,1:T(8,128)(2,1)}) %all-gather.7.cloned.1.call-update) | async-done | bytes 2097168 | tf_op jit(solution)/shard_map/all_gather | solution.py:84
  196.1 26.4 %all-gather.9.cloned.1.call-done = bf16[512,1,1024]{2,0,1:T(8,128)(2,1)} async-done(((bf16[128,1,1024]{2,0,1:T(8,128)(2,1)}), bf16[512,1,1024]{2,0,1:T(8,128)(2,1)}) %all-gather.9.cloned.1.call-update) | async-done | bytes 1048592 | tf_op jit(solution)/shard_map/all_gather | solution.py:75
  222.5 10.1 %fusion.25 = f32[512,1024]{1,0:T(8,128)} fusion(bf16[1024,1024]{0,1:T(8,128)(2,1)} %all-gather.7.cloned.1.call-done, bf16[1024,1024]{1,0:T(8,128)(2,1)} %all-gather.5.cloned.1.call-done, bf16[512,1,1024]{2,0,1:T(8,128)(2,1)} %all-gather.9.cloned.1.call-done), kind=kOutput, calls=%fused_computation.41 | convolution fusion | flops 2181562368 | bytes 7340032 | tf_op jit(solution)/shard_map/dot_general | solution.py:82
  232.6 0.0 reduce-scatter.5.cloned.1.call-update
  232.6 0.0 copy-start.9
  232.7 0.1 reshape.115
  232.8 0.4 copy.31
  233.2 0.1 copy-done.9
  233.3 0.1 broadcast_in_dim.18
  233.4 0.0 copy-start.5
  233.4 0.0 copy-start.6
  233.4 0.8 scatter_fusion
  234.2 1.2 copy.32
  235.4 34.8 %reduce-scatter.5.cloned.1.call-done = f32[128,1024]{1,0:T(8,128)} async-done(((f32[512,1024]{1,0:T(8,128)}), f32[128,1024]{1,0:T(8,128)}) %reduce-scatter.5.cloned.1.call-update) | async-done | bytes 524304 | tf_op jit(solution)/shard_map/reduce_scatter | solution.py:87
  270.2 1.3 fusion.69
  271.5 1.3 multiply_reduce_fusion
  272.8 0.9 add_convert_fusion
  (16 shorter events, 0.1 us)
Async XLA Ops:
  8.0 1.4 copy-start
  8.0 52.4 %reduce-scatter.3.cloned.1.call-start = ((), (), s32[]{:S(2)}) async-start(), calls=%async_computation.3 | async-start | bytes 2621440 | tf_op jit(solution)/shard_map/reduce_scatter | solution.py:67
  11.6 0.7 copy-start.7
  16.1 0.7 copy-start.10
  16.8 4.3 %copy-start.8 = (s32[1,1,128]{2,1,0:T(1,128)S(1)}, s32[1,1,128]{2,1,0:T(1,128)}, u32[]{:S(2)}) copy-start(s32[1,1,128]{2,1,0:T(1,128)} %param.25) | copy-start | bytes 1540
  16.8 43.6 %copy-start.2 = (bf16[512,1024]{1,0:T(8,128)(2,1)S(1)}, bf16[512,1024]{1,0:T(8,128)(2,1)}, u32[]{:S(2)}) copy-start(bf16[512,1024]{1,0:T(8,128)(2,1)} %param.14) | copy-start | bytes 3145732
  19.8 43.1 %copy-start.3 = (f32[1024]{0:T(1024)S(1)}, f32[1024]{0:T(1024)}, u32[]{:S(2)}) copy-start(f32[1024]{0:T(1024)} %param.19) | copy-start | bytes 12292
  19.8 43.1 %copy-start.4 = (f32[1024]{0:T(1024)S(1)}, f32[1024]{0:T(1024)}, u32[]{:S(2)}) copy-start(f32[1024]{0:T(1024)} %param.18) | copy-start | bytes 12292
  19.8 94.3 %all-gather.5.cloned.1.call-start = ((), (), s32[]{:S(2)}) async-start(), calls=%async_computation.4 | async-start | bytes 2113536 | tf_op jit(solution)/shard_map/all_gather | solution.py:78
  20.4 175.7 %all-gather.7.cloned.1.call-start = ((), (), s32[]{:S(2)}) async-start(), calls=%async_computation.5 | async-start | bytes 2113536 | tf_op jit(solution)/shard_map/all_gather | solution.py:84
  21.0 201.5 %all-gather.9.cloned.1.call-start = ((), (), s32[]{:S(2)}) async-start(), calls=%async_computation.7 | async-start | bytes 1310720 | tf_op jit(solution)/shard_map/all_gather | solution.py:75
  97.4 172.8 %reduce-scatter.5.cloned.1.call-start = ((), (), s32[]{:S(2)}) async-start(), calls=%async_computation.6 | async-start | bytes 2621440 | tf_op jit(solution)/shard_map/reduce_scatter | solution.py:87
  232.6 0.7 copy-start.9
  233.4 39.4 %copy-start.5 = (f32[1024]{0:T(1024)S(1)}, f32[1024]{0:T(1024)}, u32[]{:S(2)}) copy-start(f32[1024]{0:T(1024)} %param.23) | copy-start | bytes 12292
  233.4 39.4 %copy-start.6 = (f32[1024]{0:T(1024)S(1)}, f32[1024]{0:T(1024)}, u32[]{:S(2)}) copy-start(f32[1024]{0:T(1024)} %param.22) | copy-start | bytes 12292
  270.2 2.6 copy-start.1
Sparse Core Ops, SparseCore 0:
  19.9 40.4 reduce-scatter.2
  232.8 37.4 reduce-scatter.4
Sparse Core Ops, SparseCore 1:
  23.4 90.7 all-gather.4
  117.2 78.9 all-gather.6
  198.7 23.8 all-gather.8
where the time goes:
time: 282 us; the launch traced here: 281 us
  waiting for transfers between devices  200 us (71%)
  blocking collectives  30.1 us (11%)
  matrix products  18.2 us (6%)
  between operations  15.9 us (6%)
  other arithmetic  9.46 us (3%)
  local copies, waits for them, and re-layouts  7.03 us (2%)
    all_gather x1, waiting for transfers between devices, local(): lax.all_gather(down_weights, 'req', axis=1, tiled=True)  82 us
    reduce_scatter x1, waiting for transfers between devices, local(): lax.psum_scatter(partial_rows, 'grp', scatter_dimension=0, tiled=True)  39.4 us
    reduce_scatter x1, waiting for transfers between devices, local(): lax.psum_scatter(lowered_all, 'grp', scatter_dimension=0, tiled=True)  34.8 us
    all_to_all x1, blocking collectives, local(): lax.all_to_all(placed.reshape(owners, slots, width), 'req', split_axis=0,...  30.1 us
    all_gather x1, waiting for transfers between devices, local(): group_rows = lax.all_gather(even_rows, 'grp', axis=0, tiled=True)  26.4 us
    all_gather x1, waiting for transfers between devices, local(): lax.all_gather(up_weights, 'req', axis=0, tiled=True)  16.5 us
    dot_general x1, matrix products, local(): jnp.dot(activated, lax.all_gather(down_weights, 'req', axis=1, tiled=True...  10.1 us
  transfers between devices with their start and end apart: 5, of which 5 were waited for; matrix products, arithmetic and copies ran while one was open for 3% of the time, Pallas kernels for 0%

commit v1 on v0

--- a/solution.py
+++ b/solution.py
@@ -2,16 +2,43 @@
 
 import jax
 import jax.numpy as jnp
+import numpy as np
 from jax import lax
+from jax.sharding import Mesh
 from jax.sharding import PartitionSpec as P
 
 EPSILON = 1e-05
+REQ = ("rz", "ry", "rc")
 
 
 def layer_norm(values, gain, bias):
     center = values - jnp.mean(values, axis=-1, keepdims=True)
     spread = jnp.mean(center * center, axis=-1, keepdims=True)
     return center * lax.rsqrt(spread + EPSILON) * gain + bias
+
+
+def split_req(mesh):
+    column = mesh.devices[:, 0]
+    try:
+        cores = len({d.core_on_chip for d in column})
+        ys = len({d.coords[1] for d in column})
+        zs = len({d.coords[2] for d in column})
+    except AttributeError:
+        return (column.shape[0], 1, 1)
+    if zs * ys * cores != column.shape[0]:
+        return (column.shape[0], 1, 1)
+    return (zs, ys, cores)
+
+
+def gather_rows(block, first, second):
+    a = lax.all_gather(block, first, axis=0, tiled=False)
+    b = lax.all_gather(a, second, axis=0, tiled=False)
+    c = lax.all_gather(b, "rc", axis=0, tiled=False)
+    if first == "ry":
+        c = jnp.transpose(c, (1, 2, 0, 3, 4))
+    else:
+        c = jnp.transpose(c, (2, 1, 0, 3, 4))
+    return c.reshape(-1, block.shape[1])
 
 
 def local(
@@ -29,12 +56,17 @@
     row_map,
 ):
     group = lax.axis_size("grp")
-    owners = lax.axis_size("req")
+    owners = lax.axis_size(REQ)
+    zs = lax.axis_size("rz")
     rows_all = owner_slab.shape[0]
     width = owner_slab.shape[1]
     quarter = rows_all // group
     local_heads = head_weights.shape[1]
     head_dim = head_weights.shape[2] // 3
+
+    up_full = gather_rows(up_weights, "ry", "rz")
+    down_full_t = gather_rows(jnp.transpose(down_weights), "rz", "ry")
+
     projected = jnp.einsum(
         "nd,dhc->nhc", owner_slab, head_weights, preferred_element_type=jnp.float32
     ).astype(jnp.bfloat16)
@@ -68,21 +100,15 @@
     hidden = layer_norm(own_rows + mixed, first_gain, first_bias).astype(jnp.bfloat16)
     slots = quarter // owners
     placed = jnp.zeros_like(hidden).at[row_map[0, 0]].set(hidden)
-    arrived = lax.all_to_all(
-        placed.reshape(owners, slots, width), "req", split_axis=0, concat_axis=0, tiled=True
-    )
-    even_rows = arrived.reshape(quarter, width)
+    staged = placed.reshape(zs, owners // zs, slots * width)
+    staged = lax.all_to_all(staged, "rz", split_axis=0, concat_axis=0, tiled=True)
+    staged = lax.all_to_all(staged, ("ry", "rc"), split_axis=1, concat_axis=1, tiled=True)
+    even_rows = staged.reshape(quarter, width)
     group_rows = lax.all_gather(even_rows, "grp", axis=0, tiled=True)
-    raised = jnp.dot(
-        group_rows,
-        lax.all_gather(up_weights, "req", axis=0, tiled=True),
-        preferred_element_type=jnp.float32,
-    )
+    raised = jnp.dot(group_rows, up_full, preferred_element_type=jnp.float32)
     activated = jax.nn.gelu(raised, approximate=False).astype(jnp.bfloat16)
-    lowered_all = jnp.dot(
-        activated,
-        lax.all_gather(down_weights, "req", axis=1, tiled=True),
-        preferred_element_type=jnp.float32,
+    lowered_all = lax.dot_general(
+        activated, down_full_t, (((1,), (1,)), ((), ())), preferred_element_type=jnp.float32
     )
     lowered = lax.psum_scatter(lowered_all, "grp", scatter_dimension=0, tiled=True)
     layer_out = layer_norm(
@@ -96,19 +122,22 @@
 
 
 def solution(mesh):
+    zs, ys, cores = split_req(mesh)
+    devices = np.asarray(mesh.devices).reshape(zs, ys, cores, mesh.devices.shape[1])
+    inner = Mesh(devices, REQ + ("grp",))
     in_specs = (
-        P("req", None),
-        P("req", None),
+        P(REQ, None),
+        P(REQ, None),
         P(None, "grp", None),
         P("grp", None, None),
         P(),
         P(),
-        P("req", "grp"),
-        P("grp", "req"),
+        P(REQ, "grp"),
+        P("grp", REQ),
         P(),
         P(),
-        P("req", None),
-        P("req", "grp", None),
+        P(REQ, None),
+        P(REQ, "grp", None),
     )
-    out_specs = (P(("req", "grp"), None), P("req", None, "grp", None))
-    return jax.shard_map(local, mesh=mesh, in_specs=in_specs, out_specs=out_specs, check_vma=False)
+    out_specs = (P(REQ + ("grp",), None), P(REQ, None, "grp", None))
+    return jax.shard_map(local, mesh=inner, in_specs=in_specs, out_specs=out_specs, check_vma=False)

time: 282 us -> 256 us (0.908)
  waiting for transfers between devices: 200 us -> 113 us
  blocking collectives: 30.1 us -> 87.8 us
  local copies, waits for them, and re-layouts: 7.03 us -> 10.6 us
    all_gather x0 -> x2, blocking collectives: none -> 50 us  [gather_rows(): a = lax.all_gather(block, first, axis=0, tiled=False)]
    all_gather x2 -> x4, waiting for transfers between devices: 98.5 us -> 51.8 us  [the longest x2 51.6 us: gather_rows(): b = lax.all_gather(a, second, axis=0, tiled=False)]
    reduce_scatter x1, waiting for transfers between devices: 39.4 us -> 0.03 us  [local(): lax.psum_scatter(partial_rows, 'grp', scatter_dimension=0, tiled=True)]
    all_to_all x1 -> x2, blocking collectives: 30.1 us -> 37.8 us  [the longest x1 21.8 us: local(): lax.all_to_all(staged, ('ry', 'rc'), split_axis=1, concat_axis=1, tiled=T...]
    transpose x0 -> x2, local copies, waits for them, and re-layouts: none -> 6.3 us  [the longest x1 3.15 us: gather_rows(): c = jnp.transpose(c, (1, 2, 0, 3, 4))]
  transfers between devices with their start and end apart: 5 -> 7, of which waited for: 5 -> 5; matrix products, arithmetic and copies ran while one was open for 3% -> 9% of each run, Pallas kernels for 0% -> 0%
where the time goes in v1:
time: 256 us; the launch traced here: 255 us
  waiting for transfers between devices  113 us (44%)
  blocking collectives  87.8 us (34%)
  matrix products  18.1 us (7%)
  between operations  15.5 us (6%)
  local copies, waits for them, and re-layouts  10.6 us (4%)
  other arithmetic  9.59 us (4%)
    all_gather x2, waiting for transfers between devices, gather_rows(): b = lax.all_gather(a, second, axis=0, tiled=False)  51.6 us
    all_gather x2, blocking collectives, gather_rows(): a = lax.all_gather(block, first, axis=0, tiled=False)  50 us
    reduce_scatter x1, waiting for transfers between devices, local(): lax.psum_scatter(lowered_all, 'grp', scatter_dimension=0, tiled=True)  34.7 us
    all_gather x1, waiting for transfers between devices, local(): group_rows = lax.all_gather(even_rows, 'grp', axis=0, tiled=True)  26.6 us
    all_to_all x1, blocking collectives, local(): lax.all_to_all(staged, ('ry', 'rc'), split_axis=1, concat_axis=1, tiled=T...  21.8 us
    all_to_all x1, blocking collectives, local(): lax.all_to_all(staged, 'rz', split_axis=0, concat_axis=0, tiled=True)  16 us
    dot_general x1, matrix products, local(): lax.dot_general(activated, down_full_t, (((1,), (1,)), ((), ())), preferr...  10.1 us
  transfers between devices with their start and end apart: 7, of which 5 were waited for; matrix products, arithmetic and copies ran while one was open for 9% of the time, Pallas kernels for 0%

profile of v1, /device:TPU:1, one launch (start us, length us, event | category | flops | bytes accessed | tf_op | source)
XLA Modules:
  0.0 255.3 jit_solution(2603240170650563449)
XLA Ops:
  8.0 0.0 copy-start
  8.0 0.0 all-gather.14.cloned.1.call-start
  8.1 23.0 %all-gather = bf16[64,1024]{1,0:T(8,128)(2,1)} all-gather(bf16[8,1024]{1,0:T(8,128)(2,1)} %param.20), channel_id=2, replica_groups=mesh['rz'=8,'ry'=8,'rc'=2,'grp'=4] {'ry'}, dimensions={0}, use_global_device_ids=true | all-gather | bytes 147456 | tf_op jit(solution)/shard_map/all_gather | solution.py:34
  31.0 0.0 all-gather.14.cloned.1.call-update
  31.1 0.0 all-gather.18.cloned.1.call-start
  31.1 27.1 %all-gather.3 = bf16[64,1024]{1,0:T(8,128)(2,1)} all-gather(bf16[8,1024]{1,0:T(8,128)(2,1)} %bitcast.90), channel_id=5, replica_groups=mesh['rz'=8,'ry'=8,'rc'=2,'grp'=4] {'rz'}, dimensions={0}, use_global_device_ids=true | all-gather | bytes 147456 | tf_op jit(solution)/shard_map/all_gather | solution.py:34
  58.2 0.0 all-gather.18.cloned.1.call-update
  58.2 0.0 reduce-scatter.3.cloned.1.call-start
  58.3 2.2 fusion.101
  60.5 0.0 copy-start.7
  60.5 0.1 convert_element_type.25
  60.6 0.1 slice_bitcast_fusion
  60.7 0.5 copy-done.7
  61.2 3.7 %while.11 = (s32[]{:T(128)}, bf16[4,512,64]{1,2,0:T(8,128)(2,1)S(1)}, bf16[4,512,64]{1,2,0:T(8,128)(2,1)S(1)}, bf16[4,512,64]{1,2,0:T(8,128)(2,1)S(1)}, bf16[4,5...) while((s32[]{:T(128)}, bf16[4,512,64]{1,2,0:T(8,128)(2,1)S(1)}, ...), condition=%wide.region_3.4_spmd.clone, body=%wide.region_0.3_spmd.clone.sunk | while | flops 70024192 | bytes 3424341 | solution.py:93
  61.2 0.4 fusion.113
  61.6 0.2 fusion.114
  61.8 0.3 fusion.115
  62.1 0.4 fusion.113
  62.5 0.2 fusion.114
  62.7 0.3 fusion.115
  63.1 0.4 fusion.113
  63.5 0.2 fusion.114
  63.7 0.3 fusion.115
  64.0 0.4 fusion.113
  64.4 0.2 fusion.114
  64.6 0.3 fusion.115
  64.9 2.8 %convolution_bitcast_fusion = f32[512,1024]{1,0:T(8,128)} fusion(bf16[4,64,1024]{2,1,0:T(8,128)(2,1)} %param.17, bf16[4,512,64]{1,2,0:T(8,128)(2,1)S(1)} %get-tuple-element.34), kind=kOutput, calls=%fused_computation.40 | convolution fusion | flops 268435456 | bytes 2883584 | tf_op jit(solution)/shard_map/nhd,hde->ne/dot_general | solution.py:96
  67.8 0.0 reduce-scatter.3.cloned.1.call-update
  67.8 0.0 all-gather.16.cloned.1.call-start
  67.9 10.0 %all-gather.14.cloned.1.call-done = bf16[64,8,1024]{2,1,0:T(8,128)(2,1)} async-done(((bf16[8,8,1024]{2,1,0:T(8,128)(2,1)}), bf16[64,8,1024]{2,1,0:T(8,128)(2,1)}) %all-gather.14.cloned.1.call-update) | async-done | bytes 1048592 | tf_op jit(solution)/shard_map/all_gather | solution.py:35
  77.9 0.0 all-gather.16.cloned.1.call-update
  78.0 0.0 all-gather.20.cloned.1.call-start
  78.0 41.6 %all-gather.18.cloned.1.call-done = bf16[64,8,1024]{2,1,0:T(8,128)(2,1)} async-done(((bf16[8,8,1024]{2,1,0:T(8,128)(2,1)}), bf16[64,8,1024]{2,1,0:T(8,128)(2,1)}) %all-gather.18.cloned.1.call-update) | async-done | bytes 1048592 | tf_op jit(solution)/shard_map/all_gather | solution.py:35
  119.6 0.0 all-gather.20.cloned.1.call-update
  119.6 0.0 all-gather.12.cloned.1.call-start
  119.7 0.0 reduce-scatter.3.cloned.1.call-done
  119.7 1.2 fusion.64
  120.9 1.2 multiply_reduce_fusion.1
  122.2 1.9 scatter_custom_fusion
  124.1 16.0 %all_to_all.10 = bf16[8,16,1024]{2,1,0:T(8,128)(2,1)S(1)} all-to-all(bf16[8,16,1024]{2,1,0:T(8,128)(2,1)S(1)} %bitcast.87), channel_id=1, replica_groups=mesh['rz'=8,'ry'=8,'rc'=2,'grp'=4] {'rz'}, dimensions={0} | all-to-all | bytes 524288 | tf_op jit(solution)/shard_map/all_to_all | solution.py:104
  140.1 0.1 copy.42
  140.3 21.8 %all_to_all.11 = bf16[8,16,1024]{2,0,1:T(8,128)(2,1)S(1)} all-to-all(bf16[8,16,1024]{2,0,1:T(8,128)(2,1)S(1)} %copy.42), channel_id=1, replica_groups=mesh['rz'=8,'ry'=8,'rc'=2,'grp'=4] {'ry','rc'}, dimensions={1} | all-to-all | bytes 524288 | tf_op jit(solution)/shard_map/all_to_all | solution.py:105
  162.1 0.9 copy.43
  162.9 0.0 all-gather.12.cloned.1.call-update
  162.9 0.2 reduce-scatter.5.cloned.1.call-start
  163.2 0.0 all-gather.16.cloned.1.call-done
  163.2 3.2 %copy.44 = bf16[8,8,2,8,1024]{4,3,2,1,0:T(8,128)(2,1)} copy(bf16[8,8,2,8,1024]{4,3,1,0,2:T(8,128)(2,1)} %bitcast.80) | data formatting | bytes 4194304 | tf_op jit(solution)/shard_map/transpose | solution.py:38
  166.4 0.1 all-gather.20.cloned.1.call-done
  166.5 3.1 %copy.45 = bf16[8,8,2,8,1024]{4,3,2,1,0:T(8,128)(2,1)} copy(bf16[8,8,2,8,1024]{4,3,0,1,2:T(8,128)(2,1)} %bitcast.81) | data formatting | bytes 4194304 | tf_op jit(solution)/shard_map/transpose | solution.py:40
  169.6 26.6 %all-gather.12.cloned.1.call-done = bf16[512,1024]{1,0:T(8,128)(2,1)} async-done(((bf16[128,1024]{1,0:T(8,128)(2,1)}), bf16[512,1024]{1,0:T(8,128)(2,1)}) %all-gather.12.cloned.1.call-update) | async-done | bytes 1048592 | tf_op jit(solution)/shard_map/all_gather | solution.py:107
  196.3 10.1 %fusion.25 = f32[512,1024]{1,0:T(8,128)} fusion(bf16[1024,1024]{1,0:T(8,128)(2,1)} %bitcast.83, bf16[512,1024]{1,0:T(8,128)(2,1)} %all-gather.12.cloned.1.call-done, bf16[1024,1024]{1,0:T(8,128)(2,1)} %bitcast.82), kind=kOutput, calls=%fused_computation.41 | convolution fusion | flops 2181562368 | bytes 7340032 | tf_op jit(solution)/shard_map/dot_general | solution.py:110
  206.4 0.0 reduce-scatter.5.cloned.1.call-update
  206.5 0.1 reshape.123
  206.6 0.0 copy-start.1
  206.6 0.4 copy.46
  207.0 0.1 copy-done.9
  207.1 0.1 broadcast_in_dim.18
  207.2 0.0 copy-start.5
  207.2 0.8 scatter_fusion
  208.0 1.2 copy.47
  209.2 34.7 %reduce-scatter.5.cloned.1.call-done = f32[128,1024]{1,0:T(8,128)} async-done(((f32[512,1024]{1,0:T(8,128)}), f32[128,1024]{1,0:T(8,128)}) %reduce-scatter.5.cloned.1.call-update) | async-done | bytes 524304 | tf_op jit(solution)/shard_map/reduce_scatter | solution.py:113
  243.9 1.2 fusion.63
  245.0 1.2 multiply_reduce_fusion
  246.3 1.9 add_convert_fusion
  (22 shorter events, 0.1 us)
Async XLA Ops:
  8.0 50.3 %copy-start = (bf16[1024,4,192]{0,2,1:T(8,128)(2,1)S(1)}, bf16[1024,4,192]{0,2,1:T(8,128)(2,1)}, u32[]{:S(2)}) copy-start(bf16[1024,4,192]{0,2,1:T(8,128)(2,1)} %param.16) | copy-start | bytes 4718596
  8.0 69.9 %all-gather.14.cloned.1.call-start = ((), (), s32[]{:S(2)}) async-start(), calls=%async_computation.7 | async-start | bytes 1179648 | tf_op jit(solution)/shard_map/all_gather | solution.py:35
  31.1 88.5 %all-gather.18.cloned.1.call-start = ((), (), s32[]{:S(2)}) async-start(), calls=%async_computation.9 | async-start | bytes 1179648 | tf_op jit(solution)/shard_map/all_gather | solution.py:35
  58.2 61.5 %reduce-scatter.3.cloned.1.call-start = ((), (), s32[]{:S(2)}) async-start(), calls=%async_computation.4 | async-start | bytes 2621440 | tf_op jit(solution)/shard_map/reduce_scatter | solution.py:99
  60.5 0.7 copy-start.7
  67.8 51.9 %copy-start.8 = (s32[1,1,128]{2,1,0:T(1,128)S(1)}, s32[1,1,128]{2,1,0:T(1,128)}, u32[]{:S(2)}) copy-start(s32[1,1,128]{2,1,0:T(1,128)} %param.25) | copy-start | bytes 1540
  67.8 51.9 %copy-start.2 = (bf16[512,1024]{1,0:T(8,128)(2,1)S(1)}, bf16[512,1024]{1,0:T(8,128)(2,1)}, u32[]{:S(2)}) copy-start(bf16[512,1024]{1,0:T(8,128)(2,1)} %param.14) | copy-start | bytes 3145732
  67.8 54.4 %copy-start.3 = (f32[1024]{0:T(1024)S(1)}, f32[1024]{0:T(1024)}, u32[]{:S(2)}) copy-start(f32[1024]{0:T(1024)} %param.19) | copy-start | bytes 12292
  67.8 54.4 %copy-start.4 = (f32[1024]{0:T(1024)S(1)}, f32[1024]{0:T(1024)}, u32[]{:S(2)}) copy-start(f32[1024]{0:T(1024)} %param.18) | copy-start | bytes 12292
  67.8 95.4 %all-gather.16.cloned.1.call-start = ((), (), s32[]{:S(2)}) async-start(), calls=%async_computation.8 | async-start | bytes 3145728 | tf_op jit(solution)/shard_map/all_gather | solution.py:36
  78.0 88.5 %all-gather.20.cloned.1.call-start = ((), (), s32[]{:S(2)}) async-start(), calls=%async_computation.10 | async-start | bytes 3145728 | tf_op jit(solution)/shard_map/all_gather | solution.py:36
  119.6 76.6 %all-gather.12.cloned.1.call-start = ((), (), s32[]{:S(2)}) async-start(), calls=%async_computation.5 | async-start | bytes 1310720 | tf_op jit(solution)/shard_map/all_gather | solution.py:107
  162.9 80.9 %reduce-scatter.5.cloned.1.call-start = ((), (), s32[]{:S(2)}) async-start(), calls=%async_computation.6 | async-start | bytes 2621440 | tf_op jit(solution)/shard_map/reduce_scatter | solution.py:113
  206.4 0.7 copy-start.9
  206.6 37.3 %copy-start.1 = (bf16[8,16,1024]{2,1,0:T(8,128)(2,1)S(1)}, bf16[8,16,1024]{2,1,0:T(8,128)(2,1)}, u32[]{:S(2)}) copy-start(bf16[8,16,1024]{2,1,0:T(8,128)(2,1)} %copy.43) | copy-start | bytes 786436
  207.2 39.1 %copy-start.5 = (f32[1024]{0:T(1024)S(1)}, f32[1024]{0:T(1024)}, u32[]{:S(2)}) copy-start(f32[1024]{0:T(1024)} %param.23) | copy-start | bytes 12292
  207.2 39.1 %copy-start.6 = (f32[1024]{0:T(1024)S(1)}, f32[1024]{0:T(1024)}, u32[]{:S(2)}) copy-start(f32[1024]{0:T(1024)} %param.22) | copy-start | bytes 12292
Sparse Core Ops, SparseCore 0:
  31.2 46.7 all-gather.13
  80.0 39.5 all-gather.17
  121.7 22.7 all-gather.15
  146.4 20.0 all-gather.19
  169.0 27.1 all-gather.11
Sparse Core Ops, SparseCore 1:
  67.9 44.0 reduce-scatter.2
  206.5 37.3 reduce-scatter.4

commit v2 on v1

--- a/solution.py
+++ b/solution.py
@@ -30,15 +30,16 @@
     return (zs, ys, cores)
 
 
-def gather_rows(block, first, second):
-    a = lax.all_gather(block, first, axis=0, tiled=False)
-    b = lax.all_gather(a, second, axis=0, tiled=False)
-    c = lax.all_gather(b, "rc", axis=0, tiled=False)
-    if first == "ry":
-        c = jnp.transpose(c, (1, 2, 0, 3, 4))
-    else:
-        c = jnp.transpose(c, (2, 1, 0, 3, 4))
-    return c.reshape(-1, block.shape[1])
+def gather_plane(block):
+    return lax.all_gather(block, ("rz", "ry"), axis=0, tiled=False)
+
+
+def swap_cores(plane):
+    other = lax.ppermute(plane, "rc", [(0, 1), (1, 0)])
+    mine = lax.axis_index("rc")
+    cores = jnp.arange(2, dtype=jnp.int32).reshape(1, 2, 1, 1)
+    whole = jnp.where(cores == mine, plane[:, None], other[:, None])
+    return whole.reshape(-1, plane.shape[-1])
 
 
 def local(
@@ -57,15 +58,14 @@
 ):
     group = lax.axis_size("grp")
     owners = lax.axis_size(REQ)
-    zs = lax.axis_size("rz")
     rows_all = owner_slab.shape[0]
     width = owner_slab.shape[1]
     quarter = rows_all // group
     local_heads = head_weights.shape[1]
     head_dim = head_weights.shape[2] // 3
 
-    up_full = gather_rows(up_weights, "ry", "rz")
-    down_full_t = gather_rows(jnp.transpose(down_weights), "rz", "ry")
+    up_plane = gather_plane(up_weights)
+    down_plane = gather_plane(jnp.transpose(down_weights))
 
     projected = jnp.einsum(
         "nd,dhc->nhc", owner_slab, head_weights, preferred_element_type=jnp.float32
@@ -100,11 +100,16 @@
     hidden = layer_norm(own_rows + mixed, first_gain, first_bias).astype(jnp.bfloat16)
     slots = quarter // owners
     placed = jnp.zeros_like(hidden).at[row_map[0, 0]].set(hidden)
-    staged = placed.reshape(zs, owners // zs, slots * width)
-    staged = lax.all_to_all(staged, "rz", split_axis=0, concat_axis=0, tiled=True)
-    staged = lax.all_to_all(staged, ("ry", "rc"), split_axis=1, concat_axis=1, tiled=True)
-    even_rows = staged.reshape(quarter, width)
-    group_rows = lax.all_gather(even_rows, "grp", axis=0, tiled=True)
+    arrived = lax.all_to_all(
+        placed.reshape(owners, slots, width), REQ, split_axis=0, concat_axis=0, tiled=True
+    )
+    even_rows = arrived.reshape(quarter, width)
+    up_plane, down_plane, _ = lax.optimization_barrier((up_plane, down_plane, even_rows))
+    up_full = swap_cores(up_plane)
+    down_full_t = swap_cores(down_plane)
+    copies = jnp.broadcast_to(even_rows[None], (group, quarter, width))
+    group_rows = lax.all_to_all(copies, "grp", split_axis=0, concat_axis=0, tiled=True)
+    group_rows = group_rows.reshape(group * quarter, width)
     raised = jnp.dot(group_rows, up_full, preferred_element_type=jnp.float32)
     activated = jax.nn.gelu(raised, approximate=False).astype(jnp.bfloat16)
     lowered_all = lax.dot_general(

time: 256 us -> 271 us (1.059)
  blocking collectives: 87.8 us -> 30.1 us
  waiting for transfers between devices: 113 us -> 169 us
  starting transfers between devices: 0.46 us -> 13.9 us
  other arithmetic: 9.59 us -> 15.4 us
  local copies, waits for them, and re-layouts: 10.6 us -> 7.63 us
    all_gather x2 -> x0, blocking collectives: 50 us -> none  [gather_rows(): a = lax.all_gather(block, first, axis=0, tiled=False)]
    reduce_scatter x1, waiting for transfers between devices: 0.03 us -> 39.4 us  [local(): lax.psum_scatter(partial_rows, 'grp', scatter_dimension=0, tiled=True)]
    all_gather x5 -> x2, waiting for transfers between devices: 78.4 us -> 92.2 us  [gather_plane(): return lax.all_gather(block, ('rz', 'ry'), axis=0, tiled=False)]
    ppermute x0 -> x2, starting transfers between devices: none -> 9.25 us  [swap_cores(): other = lax.ppermute(plane, 'rc', [(0, 1), (1, 0)])]
    all_to_all x0 -> x1, waiting for transfers between devices: none -> 8.33 us  [local(): lax.all_to_all(copies, 'grp', split_axis=0, concat_axis=0, tiled=True)]
    all_to_all x2 -> x1, blocking collectives: 37.8 us -> 30.1 us  [local(): lax.all_to_all(placed.reshape(owners, slots, width), REQ, split_axis=0, c...]
    reduce_scatter x1, waiting for transfers between devices: 34.7 us -> 28.1 us  [local(): lax.psum_scatter(lowered_all, 'grp', scatter_dimension=0, tiled=True)]
    transpose x2 -> x0, local copies, waits for them, and re-layouts: 6.3 us -> none  [the longest x1 3.15 us: gather_rows(): c = jnp.transpose(c, (1, 2, 0, 3, 4))]
  transfers between devices with their start and end apart: 7 -> 7, of which waited for: 5 -> 5; matrix products, arithmetic and copies ran while one was open for 9% -> 6% of each run, Pallas kernels for 0% -> 0%
where the time goes in v2:
time: 271 us; the launch traced here: 270 us
  waiting for transfers between devices  169 us (62%)
  blocking collectives  30.1 us (11%)
  matrix products  18.2 us (7%)
  between operations  15.8 us (6%)
  other arithmetic  15.4 us (6%)
  starting transfers between devices  13.9 us (5%)
  local copies, waits for them, and re-layouts  7.63 us (3%)
    all_gather x2, waiting for transfers between devices, gather_plane(): return lax.all_gather(block, ('rz', 'ry'), axis=0, tiled=False)  92.2 us
    reduce_scatter x1, waiting for transfers between devices, local(): lax.psum_scatter(partial_rows, 'grp', scatter_dimension=0, tiled=True)  39.4 us
    all_to_all x1, blocking collectives, local(): lax.all_to_all(placed.reshape(owners, slots, width), REQ, split_axis=0, c...  30.1 us
    reduce_scatter x1, waiting for transfers between devices, local(): lax.psum_scatter(lowered_all, 'grp', scatter_dimension=0, tiled=True)  28.1 us
    dot_general x1, matrix products, local(): lax.dot_general(activated, down_full_t, (((1,), (1,)), ((), ())), preferr...  10.1 us
    ppermute x2, starting transfers between devices, swap_cores(): other = lax.ppermute(plane, 'rc', [(0, 1), (1, 0)])  9.25 us
    all_to_all x1, waiting for transfers between devices, local(): lax.all_to_all(copies, 'grp', split_axis=0, concat_axis=0, tiled=True)  8.33 us
    select_n x2, other arithmetic, swap_cores(): whole = jnp.where(cores == mine, plane[:, None], other[:, None])  5.93 us
  transfers between devices with their start and end apart: 7, of which 5 were waited for; matrix products, arithmetic and copies ran while one was open for 6% of the time, Pallas kernels for 0%

profile of v2, /device:TPU:1, one launch (start us, length us, event | category | flops | bytes accessed | tf_op | source)
XLA Modules:
  0.0 270.2 jit_solution(10769040261524625001)
XLA Ops:
  8.0 0.0 copy-start
  8.0 0.0 reduce-scatter.3.cloned.1.call-start
  8.1 1.3 copy-done
  9.4 2.2 fusion.101
  11.6 0.0 copy-start.8
  11.7 0.1 convert_element_type.25
  11.8 0.1 slice_bitcast_fusion
  11.9 0.5 copy-done.8
  12.3 3.7 %while.11 = (s32[]{:T(128)}, bf16[4,512,64]{1,2,0:T(8,128)(2,1)S(1)}, bf16[4,512,64]{1,2,0:T(8,128)(2,1)S(1)}, bf16[4,512,64]{1,2,0:T(8,128)(2,1)S(1)}, bf16[4,5...) while((s32[]{:T(128)}, bf16[4,512,64]{1,2,0:T(8,128)(2,1)S(1)}, ...), condition=%wide.region_3.4_spmd.clone, body=%wide.region_0.3_spmd.clone.sunk | while | flops 70024192 | bytes 3424341 | solution.py:93
  12.3 0.4 fusion.113
  12.7 0.2 fusion.114
  12.9 0.3 fusion.115
  13.3 0.4 fusion.113
  13.7 0.2 fusion.114
  13.9 0.3 fusion.115
  14.2 0.4 fusion.113
  14.6 0.2 fusion.114
  14.8 0.3 fusion.115
  15.1 0.4 fusion.113
  15.6 0.2 fusion.114
  15.8 0.3 fusion.115
  16.1 0.0 copy-start.11
  16.1 0.7 copy-done.11
  16.8 3.0 %convolution_bitcast_fusion = f32[512,1024]{1,0:T(8,128)} fusion(bf16[4,64,1024]{2,1,0:T(8,128)(2,1)} %param.17, bf16[4,512,64]{1,2,0:T(8,128)(2,1)} %copy-done.11), kind=kOutput, calls=%fused_computation.42 | convolution fusion | flops 268435456 | bytes 2883584 | tf_op jit(solution)/shard_map/nhd,hde->ne/dot_general | solution.py:96
  19.8 0.0 reduce-scatter.3.cloned.1.call-update
  19.8 0.0 all-gather.5.cloned.1.call-start
  19.9 0.5 all-gather.5.cloned.1.call-update
  20.4 0.0 all-gather.7.cloned.1.call-start
  20.5 0.5 all-gather.7.cloned.1.call-update
  21.0 39.4 %reduce-scatter.3.cloned.1.call-done = f32[128,1024]{1,0:T(8,128)} async-done(((f32[512,1024]{1,0:T(8,128)}), f32[128,1024]{1,0:T(8,128)}) %reduce-scatter.3.cloned.1.call-update) | async-done | bytes 524304 | tf_op jit(solution)/shard_map/reduce_scatter | solution.py:99
  60.4 1.2 fusion.64
  61.6 1.2 multiply_reduce_fusion.1
  62.9 1.9 scatter_custom_fusion
  64.8 0.5 broadcast.151
  65.3 0.8 reduce
  66.1 0.2 reshape.183
  66.3 30.1 %all_to_all.10 = bf16[128,2,512]{2,1,0:T(2,128)(2,1)S(1)} all-to-all(bf16[128,2,512]{2,1,0:T(2,128)(2,1)S(1)} %reshape.183), channel_id=1, replica_groups=mesh['rz'=8,'ry'=8,'rc'=2,'grp'=4] {'rz','ry','rc'}, dimensions={0} | all-to-all | bytes 524288 | tf_op jit(solution)/shard_map/all_to_all | solution.py:103
  96.4 0.2 reshape.184
  96.7 0.1 copy.46
  96.7 12.0 %all-gather.5.cloned.1.call-done = bf16[512,1024]{1,0:T(8,128)(2,1)} async-done(((bf16[8,1024]{1,0:T(8,128)(2,1)}), bf16[512,1024]{1,0:T(8,128)(2,1)}) %all-gather.5.cloned.1.call-update) | async-done | bytes 1048592 | tf_op jit(solution)/shard_map/all_gather | solution.py:34
  108.7 80.2 %all-gather.7.cloned.1.call-done = bf16[512,1024]{1,0:T(8,128)(2,1)} async-done(((bf16[8,1024]{1,0:T(8,128)(2,1)}), bf16[512,1024]{1,0:T(8,128)(2,1)}) %all-gather.7.cloned.1.call-update) | async-done | bytes 1048592 | tf_op jit(solution)/shard_map/all_gather | solution.py:34
  188.9 7.3 %collective-permute-start.1 = (bf16[64,8,1024]{2,1,0:T(8,128)(2,1)}, bf16[64,8,1024]{2,1,0:T(8,128)(2,1)}, u32[]{:S(2)}, u32[]{:S(2)}) collective-permute-start(bf16[64,8,1024]{2,1,0:T(8,128)(2,1)} %bitcast.84), channel_id=1, source_target_pairs={{0,4},{4,0},{1,5},{5,1},{2,6},{6,2},{3,7},{7,3},{8,12},{12,8},{9,1... | collective-permute-start | bytes 3145736 | tf_op jit(solution)/shard_map/ppermute | solution.py:38
  196.3 1.9 collective-permute-start
  198.2 1.1 broadcast_in_dim.89
  199.3 4.3 %all-to-all-start.1 = ((bf16[4,128,1024]{2,1,0:T(8,128)(2,1)}), bf16[4,128,1024]{2,1,0:T(8,128)(2,1)}, u32[]{:S(2)}, u32[]{:S(2)}) async-start(bf16[4,128,1024]{2,1,0:T(8,128)(2,1)} %broadcast_in_dim.89), calls=%async_computation.2 | async-start | bytes 2097152 | tf_op jit(solution)/shard_map/all_to_all | solution.py:111
  203.6 0.2 reduce-scatter.5.cloned.1.call-start
  203.8 0.1 broadcast_in_dim.93
  203.9 0.1 broadcast_in_dim.94
  204.0 3.2 %bitcast_select_fusion = bf16[1024,1024]{1,0:T(8,128)(2,1)} fusion(pred[1024]{0:T(1024)(128)(4,1)S(1)} %broadcast_in_dim.94, bf16[64,8,1024]{2,1,0:T(8,128)(2,1)} %collective-permute-done.1, bf16[64,8,1024]{2,1,0:T(8,128)(2,1)} %bitcast.85), kind=kLoop, calls=%fused_computation.25 | loop fusion | flops 1048576 | bytes 4195328 | tf_op jit(solution)/shard_map/jit(_where)/select_n | solution.py:41
  207.2 2.7 %broadcast_select_fusion = bf16[64,2,8,1024]{3,2,1,0:T(8,128)(2,1)} fusion(pred[2]{0:T(512)(128)(4,1)S(1)} %iota_compare_fusion.1, bf16[64,8,1024]{2,1,0:T(8,128)(2,1)} %collective-permute-done, bf16[64,8,1024]{2,1,0:T(8,128)(2,1)S(1)} %bitcast.83), kind=kLoop, calls=%fused_computation.39 | loop fusion | flops 1048576 | bytes 4194306 | tf_op jit(solution)/shard_map/jit(_where)/select_n | solution.py:41
  210.0 8.3 %all-to-all-done.1 = bf16[4,128,1024]{2,1,0:T(8,128)(2,1)} async-done(((bf16[4,128,1024]{2,1,0:T(8,128)(2,1)}), bf16[4,128,1024]{2,1,0:T(8,128)(2,1)}, u32[]{:S(2)}, u32[]{:S(2)}) %all-to-all-start.1) | async-done | bytes 1048608 | tf_op jit(solution)/shard_map/all_to_all | solution.py:111
  218.3 10.1 %fusion.25 = f32[512,1024]{1,0:T(8,128)} fusion(bf16[1024,1024]{1,0:T(8,128)(2,1)} %bitcast_select_fusion, bf16[512,1024]{1,0:T(8,128)(2,1)} %bitcast.11, bf16[1024,1024]{1,0:T(8,128)(2,1)} %bitcast.80), kind=kOutput, calls=%fused_computation.43 | convolution fusion | flops 2181562368 | bytes 7340032 | tf_op jit(solution)/shard_map/dot_general | solution.py:115
  228.4 0.0 reduce-scatter.5.cloned.1.call-update
  228.4 0.0 copy-start.10
  228.5 0.1 reshape.172
  228.6 0.4 copy.33
  229.0 0.1 copy-done.10
  229.1 0.1 broadcast_in_dim.100
  229.2 0.8 scatter_fusion
  230.0 1.2 copy.34
  231.2 28.1 %reduce-scatter.5.cloned.1.call-done = f32[128,1024]{1,0:T(8,128)} async-done(((f32[512,1024]{1,0:T(8,128)}), f32[128,1024]{1,0:T(8,128)}) %reduce-scatter.5.cloned.1.call-update) | async-done | bytes 524304 | tf_op jit(solution)/shard_map/reduce_scatter | solution.py:118
  259.3 1.3 fusion.63
  260.6 1.3 multiply_reduce_fusion
  261.9 0.9 add_convert_fusion
  (27 shorter events, 0.1 us)
Async XLA Ops:
  8.0 1.4 copy-start
  8.0 52.4 %reduce-scatter.3.cloned.1.call-start = ((), (), s32[]{:S(2)}) async-start(), calls=%async_computation.4 | async-start | bytes 2621440 | tf_op jit(solution)/shard_map/reduce_scatter | solution.py:99
  11.6 0.7 copy-start.8
  16.1 0.7 copy-start.11
  16.8 4.2 %copy-start.9 = (s32[1,1,128]{2,1,0:T(1,128)S(1)}, s32[1,1,128]{2,1,0:T(1,128)}, u32[]{:S(2)}) copy-start(s32[1,1,128]{2,1,0:T(1,128)} %param.25) | copy-start | bytes 1540
  16.8 43.6 %copy-start.3 = (bf16[512,1024]{1,0:T(8,128)(2,1)S(1)}, bf16[512,1024]{1,0:T(8,128)(2,1)}, u32[]{:S(2)}) copy-start(bf16[512,1024]{1,0:T(8,128)(2,1)} %param.14) | copy-start | bytes 3145732
  19.8 43.1 %copy-start.4 = (f32[1024]{0:T(1024)S(1)}, f32[1024]{0:T(1024)}, u32[]{:S(2)}) copy-start(f32[1024]{0:T(1024)} %param.19) | copy-start | bytes 12292
  19.8 43.1 %copy-start.5 = (f32[1024]{0:T(1024)S(1)}, f32[1024]{0:T(1024)}, u32[]{:S(2)}) copy-start(f32[1024]{0:T(1024)} %param.18) | copy-start | bytes 12292
  19.8 88.9 %all-gather.5.cloned.1.call-start = ((), (), s32[]{:S(2)}) async-start(), calls=%async_computation.6 | async-start | bytes 1064960 | tf_op jit(solution)/shard_map/all_gather | solution.py:34
  20.4 168.5 %all-gather.7.cloned.1.call-start = ((), (), s32[]{:S(2)}) async-start(), calls=%async_computation.7 | async-start | bytes 1064960 | tf_op jit(solution)/shard_map/all_gather | solution.py:34
  188.9 15.1 %collective-permute-start.1 = (bf16[64,8,1024]{2,1,0:T(8,128)(2,1)}, bf16[64,8,1024]{2,1,0:T(8,128)(2,1)}, u32[]{:S(2)}, u32[]{:S(2)}) collective-permute-start(bf16[64,8,1024]{2,1,0:T(8,128)(2,1)} %bitcast.84), channel_id=1, source_target_pairs={{0,4},{4,0},{1,5},{5,1},{2,6},{6,2},{3,7},{7,3},{8,12},{12,8},{9,1... | collective-permute-start | bytes 3145736 | tf_op jit(solution)/shard_map/ppermute | solution.py:38
  196.3 11.0 %collective-permute-start = (bf16[64,8,1024]{2,1,0:T(8,128)(2,1)}, bf16[64,8,1024]{2,1,0:T(8,128)(2,1)}, u32[]{:S(2)}, u32[]{:S(2)}) collective-permute-start(bf16[64,8,1024]{2,1,0:T(8,128)(2,1)} %bitcast.82), channel_id=1, source_target_pairs={{0,4},{4,0},{1,5},{5,1},{2,6},{6,2},{3,7},{7,3},{8,12},{12,8},{9,1... | collective-permute-start | bytes 3145736 | tf_op jit(solution)/shard_map/ppermute | solution.py:38
  199.3 19.0 %all-to-all-start.1 = ((bf16[4,128,1024]{2,1,0:T(8,128)(2,1)}), bf16[4,128,1024]{2,1,0:T(8,128)(2,1)}, u32[]{:S(2)}, u32[]{:S(2)}) async-start(bf16[4,128,1024]{2,1,0:T(8,128)(2,1)} %broadcast_in_dim.89), calls=%async_computation.2 | async-start | bytes 2097152 | tf_op jit(solution)/shard_map/all_to_all | solution.py:111
  203.6 55.8 %reduce-scatter.5.cloned.1.call-start = ((), (), s32[]{:S(2)}) async-start(), calls=%async_computation.5 | async-start | bytes 2621440 | tf_op jit(solution)/shard_map/reduce_scatter | solution.py:118
  204.0 3.2 %copy-start.2 = (bf16[512,1024]{1,0:T(8,128)(2,1)S(1)}, bf16[512,1024]{1,0:T(8,128)(2,1)}, u32[]{:S(2)}) copy-start(bf16[512,1024]{1,0:T(8,128)(2,1)} %all-gather.5.cloned.1.call-done) | copy-start | bytes 3145732
  228.4 0.7 copy-start.10
  229.2 32.7 %copy-start.6 = (f32[1024]{0:T(1024)S(1)}, f32[1024]{0:T(1024)}, u32[]{:S(2)}) copy-start(f32[1024]{0:T(1024)} %param.23) | copy-start | bytes 12292
  229.2 32.7 %copy-start.7 = (f32[1024]{0:T(1024)S(1)}, f32[1024]{0:T(1024)}, u32[]{:S(2)}) copy-start(f32[1024]{0:T(1024)} %param.22) | copy-start | bytes 12292
  259.3 2.6 copy-start.1
Sparse Core Ops, SparseCore 0:
  20.0 40.4 reduce-scatter.2
  228.5 30.7 reduce-scatter.4
Sparse Core Ops, SparseCore 1:
  23.4 85.3 all-gather.4
  111.6 77.2 all-gather.6
